TPU v7x, 256 devices: a whole 4x4x8 slice. The times are simulated.
256 devices in a mesh: ctx: 32 (over z, x), tp: 8 (over y, core).
Axes of the slice: x: 4, y: 4, z: 8, core: 2. Of those that a mesh axis runs over, the one named last changes fastest.
Arguments:
- tokens: bfloat16 [16384, 3072], P(('ctx', 'tp')), may hold values from -6 to 6
- w_query: bfloat16 [3072, 4096], P(None, 'tp'), may hold values from -0.109375 to 0.109375
- w_key: bfloat16 [3072, 4096], P(None, 'tp'), may hold values from -0.109375 to 0.109375
- w_value: bfloat16 [3072, 4096], P(None, 'tp'), may hold values from -0.109375 to 0.109375
- norm_gain: float32 [4096], P('tp'), may hold values from 0.1 to 1.9
Outputs:
- attended: bfloat16 [16384, 4096], P('ctx', 'tp')
All inputs are finite; a program needn't handle non-finite values.
Results may differ from a plain program's by a relative error of at most 0.0062.
Values may be sent and summed in bfloat16 or wider, within the bound.
No kernel may reach another device: no remote copies, remote signals or barrier semaphores. Data moves between devices by JAX's collectives and lax.ppermute only.
A program may use at most 64 MiB of HBM per device.

v0:
```python
import jax
import jax.numpy as jnp
from jax import lax
from jax.sharding import PartitionSpec as P

HEAD_DIM = 128
BLOCK = 512
EPSILON = 1e-06


def from_behind(value, axis, by):
    size = lax.axis_size(axis)
    pairs = [(i, i + by) for i in range(size) if 0 <= i + by < size]
    return lax.ppermute(value, axis, pairs)


def body(tokens, w_query, w_key, w_value, norm_gain):
    local_width = w_query.shape[1]
    head_count = local_width // HEAD_DIM
    piece_rows = lax.all_gather(tokens, "tp", axis=0, tiled=True)
    query_part = jnp.dot(piece_rows, w_query, preferred_element_type=jnp.float32).astype(
        jnp.bfloat16
    )
    key_part = jnp.dot(piece_rows, w_key, preferred_element_type=jnp.float32).astype(jnp.bfloat16)
    value_part = jnp.dot(piece_rows, w_value, preferred_element_type=jnp.float32).astype(
        jnp.bfloat16
    )
    projected = jnp.concatenate([query_part, key_part, value_part], axis=1)
    group_len = projected.shape[0]
    block_count = group_len // BLOCK
    shaped = projected.reshape(block_count, BLOCK, 3, head_count, HEAD_DIM)
    query_rows = shaped[:, :, 0]
    key_rows = shaped[:, :, 1]
    value_rows = shaped[:, :, 2]
    block_states = jnp.einsum(
        "bshd,bshe->bhde", key_rows, value_rows, preferred_element_type=jnp.float32
    )
    local_state = jnp.sum(block_states, axis=0)
    empty_state = jnp.zeros_like(local_state)

    def advance(step_index, carried):
        return from_behind(carried + local_state, "ctx", 1)

    prefix_state = lax.fori_loop(0, lax.axis_size("ctx") - 1, advance, empty_state)
    running = jnp.cumsum(block_states, axis=0)
    earlier = jnp.concatenate([jnp.zeros_like(block_states), running[:-1]], axis=0)
    block_start = prefix_state[None] + earlier
    scores = jnp.einsum("bqhd,bkhd->bhqk", query_rows, key_rows, preferred_element_type=jnp.float32)
    causal = jnp.arange(BLOCK)[:, None] >= jnp.arange(BLOCK)[None, :]
    scores = jnp.where(causal[None, None], scores, jnp.float32(0.0)).astype(jnp.bfloat16)
    inner = jnp.einsum("bhqk,bkhe->bqhe", scores, value_rows, preferred_element_type=jnp.float32)
    carried_part = jnp.einsum(
        "bqhd,bhde->bqhe",
        query_rows.astype(jnp.float32),
        block_start,
        precision=lax.Precision.HIGHEST,
    )
    mixed = inner + carried_part
    mean_square = jnp.mean(mixed * mixed, axis=-1, keepdims=True)
    normed = mixed * lax.rsqrt(mean_square + EPSILON) * norm_gain.reshape(head_count, HEAD_DIM)
    return normed.reshape(group_len, local_width).astype(jnp.bfloat16)


def solution(mesh):
    placed = (P(("ctx", "tp"), None), P(None, "tp"), P(None, "tp"), P(None, "tp"), P("tp"))
    return jax.shard_map(
        body, mesh=mesh, in_specs=placed, out_specs=P("ctx", "tp"), check_vma=False
    )
```

profile of v0, /device:TPU:128, one launch (start us, length us, event | category | flops | bytes accessed | tf_op | source)
XLA Modules:
  0.0 505.0 jit_solution(23542777974359117)
XLA Ops:
  8.0 32.9 %all-gather.2.cloned.1.call-done = bf16[512,3072]{1,0:T(8,128)(2,1)} async-done(((bf16[64,3072]{1,0:T(8,128)(2,1)}), bf16[512,3072]{1,0:T(8,128)(2,1)}) %all-gather.2.cloned.1.call-update) | async-done | bytes 3145744 | tf_op jit(solution)/shard_map/all_gather | solution.py:20
  41.0 3.9 convolution_convert_fusion
  50.9 436.2 %while.10 = (s32[]{:T(128)}, f32[4,128,128]{2,1,0:T(8,128)S(1)}, f32[4,128,128]{2,1,0:T(8,128)}, s32[]{:T(128)}) while((s32[]{:T(128)}, f32[4,128,128]{2,1,0:T(8,128)S(1)}, f32[4,128,128]{2,1,0:T(8,128)}, s32[]{:T(128)}) %tuple.19), condition=%wide.region_1.0_spmd, body=%wide.region_0.0_spmd.sunk | while | flops 65538 | bytes 1835101 | solution.py:44
  52.6 3.4 collective-permute-start
  56.0 10.5 %collective-permute-done = f32[4,128,128]{2,1,0:T(8,128)S(1)} collective-permute-done((f32[4,128,128]{2,1,0:T(8,128)}, f32[4,128,128]{2,1,0:T(8,128)S(1)}, u32[]{:S(2)}, u32[]{:S(2)}) %collective-permute-start) | collective-permute-done | bytes 262176 | tf_op jit(solution)/shard_map/while/body/eval_jaxpr/ppermute | solution.py:14
  68.1 1.9 collective-permute-start
  70.0 11.1 %collective-permute-done = f32[4,128,128]{2,1,0:T(8,128)S(1)} collective-permute-done((f32[4,128,128]{2,1,0:T(8,128)}, f32[4,128,128]{2,1,0:T(8,128)S(1)}, u32[]{:S(2)}, u32[]{:S(2)}) %collective-permute-start) | collective-permute-done | bytes 262176 | tf_op jit(solution)/shard_map/while/body/eval_jaxpr/ppermute | solution.py:14
  84.7 10.2 %collective-permute-done = f32[4,128,128]{2,1,0:T(8,128)S(1)} collective-permute-done((f32[4,128,128]{2,1,0:T(8,128)}, f32[4,128,128]{2,1,0:T(8,128)S(1)}, u32[]{:S(2)}, u32[]{:S(2)}) %collective-permute-start) | collective-permute-done | bytes 262176 | tf_op jit(solution)/shard_map/while/body/eval_jaxpr/ppermute | solution.py:14
  98.5 9.9 %collective-permute-done = f32[4,128,128]{2,1,0:T(8,128)S(1)} collective-permute-done((f32[4,128,128]{2,1,0:T(8,128)}, f32[4,128,128]{2,1,0:T(8,128)S(1)}, u32[]{:S(2)}, u32[]{:S(2)}) %collective-permute-start) | collective-permute-done | bytes 262176 | tf_op jit(solution)/shard_map/while/body/eval_jaxpr/ppermute | solution.py:14
  110.1 1.9 collective-permute-start
  112.0 9.9 %collective-permute-done = f32[4,128,128]{2,1,0:T(8,128)S(1)} collective-permute-done((f32[4,128,128]{2,1,0:T(8,128)}, f32[4,128,128]{2,1,0:T(8,128)S(1)}, u32[]{:S(2)}, u32[]{:S(2)}) %collective-permute-start) | collective-permute-done | bytes 262176 | tf_op jit(solution)/shard_map/while/body/eval_jaxpr/ppermute | solution.py:14
  123.5 1.9 collective-permute-start
  125.4 9.9 %collective-permute-done = f32[4,128,128]{2,1,0:T(8,128)S(1)} collective-permute-done((f32[4,128,128]{2,1,0:T(8,128)}, f32[4,128,128]{2,1,0:T(8,128)S(1)}, u32[]{:S(2)}, u32[]{:S(2)}) %collective-permute-start) | collective-permute-done | bytes 262176 | tf_op jit(solution)/shard_map/while/body/eval_jaxpr/ppermute | solution.py:14
  137.0 1.9 collective-permute-start
  138.9 9.9 %collective-permute-done = f32[4,128,128]{2,1,0:T(8,128)S(1)} collective-permute-done((f32[4,128,128]{2,1,0:T(8,128)}, f32[4,128,128]{2,1,0:T(8,128)S(1)}, u32[]{:S(2)}, u32[]{:S(2)}) %collective-permute-start) | collective-permute-done | bytes 262176 | tf_op jit(solution)/shard_map/while/body/eval_jaxpr/ppermute | solution.py:14
  150.4 1.9 collective-permute-start
  152.3 9.9 %collective-permute-done = f32[4,128,128]{2,1,0:T(8,128)S(1)} collective-permute-done((f32[4,128,128]{2,1,0:T(8,128)}, f32[4,128,128]{2,1,0:T(8,128)S(1)}, u32[]{:S(2)}, u32[]{:S(2)}) %collective-permute-start) | collective-permute-done | bytes 262176 | tf_op jit(solution)/shard_map/while/body/eval_jaxpr/ppermute | solution.py:14
  163.9 1.9 collective-permute-start
  165.8 9.9 %collective-permute-done = f32[4,128,128]{2,1,0:T(8,128)S(1)} collective-permute-done((f32[4,128,128]{2,1,0:T(8,128)}, f32[4,128,128]{2,1,0:T(8,128)S(1)}, u32[]{:S(2)}, u32[]{:S(2)}) %collective-permute-start) | collective-permute-done | bytes 262176 | tf_op jit(solution)/shard_map/while/body/eval_jaxpr/ppermute | solution.py:14
  179.3 10.6 %collective-permute-done = f32[4,128,128]{2,1,0:T(8,128)S(1)} collective-permute-done((f32[4,128,128]{2,1,0:T(8,128)}, f32[4,128,128]{2,1,0:T(8,128)S(1)}, u32[]{:S(2)}, u32[]{:S(2)}) %collective-permute-start) | collective-permute-done | bytes 262176 | tf_op jit(solution)/shard_map/while/body/eval_jaxpr/ppermute | solution.py:14
  191.5 1.9 collective-permute-start
  193.4 11.7 %collective-permute-done = f32[4,128,128]{2,1,0:T(8,128)S(1)} collective-permute-done((f32[4,128,128]{2,1,0:T(8,128)}, f32[4,128,128]{2,1,0:T(8,128)S(1)}, u32[]{:S(2)}, u32[]{:S(2)}) %collective-permute-start) | collective-permute-done | bytes 262176 | tf_op jit(solution)/shard_map/while/body/eval_jaxpr/ppermute | solution.py:14
  206.8 1.9 collective-permute-start
  208.7 12.5 %collective-permute-done = f32[4,128,128]{2,1,0:T(8,128)S(1)} collective-permute-done((f32[4,128,128]{2,1,0:T(8,128)}, f32[4,128,128]{2,1,0:T(8,128)S(1)}, u32[]{:S(2)}, u32[]{:S(2)}) %collective-permute-start) | collective-permute-done | bytes 262176 | tf_op jit(solution)/shard_map/while/body/eval_jaxpr/ppermute | solution.py:14
  222.9 1.9 collective-permute-start
  224.8 11.6 %collective-permute-done = f32[4,128,128]{2,1,0:T(8,128)S(1)} collective-permute-done((f32[4,128,128]{2,1,0:T(8,128)}, f32[4,128,128]{2,1,0:T(8,128)S(1)}, u32[]{:S(2)}, u32[]{:S(2)}) %collective-permute-start) | collective-permute-done | bytes 262176 | tf_op jit(solution)/shard_map/while/body/eval_jaxpr/ppermute | solution.py:14
  240.0 10.8 %collective-permute-done = f32[4,128,128]{2,1,0:T(8,128)S(1)} collective-permute-done((f32[4,128,128]{2,1,0:T(8,128)}, f32[4,128,128]{2,1,0:T(8,128)S(1)}, u32[]{:S(2)}, u32[]{:S(2)}) %collective-permute-start) | collective-permute-done | bytes 262176 | tf_op jit(solution)/shard_map/while/body/eval_jaxpr/ppermute | solution.py:14
  254.4 9.9 %collective-permute-done = f32[4,128,128]{2,1,0:T(8,128)S(1)} collective-permute-done((f32[4,128,128]{2,1,0:T(8,128)}, f32[4,128,128]{2,1,0:T(8,128)S(1)}, u32[]{:S(2)}, u32[]{:S(2)}) %collective-permute-start) | collective-permute-done | bytes 262176 | tf_op jit(solution)/shard_map/while/body/eval_jaxpr/ppermute | solution.py:14
  267.9 9.9 %collective-permute-done = f32[4,128,128]{2,1,0:T(8,128)S(1)} collective-permute-done((f32[4,128,128]{2,1,0:T(8,128)}, f32[4,128,128]{2,1,0:T(8,128)S(1)}, u32[]{:S(2)}, u32[]{:S(2)}) %collective-permute-start) | collective-permute-done | bytes 262176 | tf_op jit(solution)/shard_map/while/body/eval_jaxpr/ppermute | solution.py:14
  281.3 9.9 %collective-permute-done = f32[4,128,128]{2,1,0:T(8,128)S(1)} collective-permute-done((f32[4,128,128]{2,1,0:T(8,128)}, f32[4,128,128]{2,1,0:T(8,128)S(1)}, u32[]{:S(2)}, u32[]{:S(2)}) %collective-permute-start) | collective-permute-done | bytes 262176 | tf_op jit(solution)/shard_map/while/body/eval_jaxpr/ppermute | solution.py:14
  294.8 9.9 %collective-permute-done = f32[4,128,128]{2,1,0:T(8,128)S(1)} collective-permute-done((f32[4,128,128]{2,1,0:T(8,128)}, f32[4,128,128]{2,1,0:T(8,128)S(1)}, u32[]{:S(2)}, u32[]{:S(2)}) %collective-permute-start) | collective-permute-done | bytes 262176 | tf_op jit(solution)/shard_map/while/body/eval_jaxpr/ppermute | solution.py:14
  308.3 9.9 %collective-permute-done = f32[4,128,128]{2,1,0:T(8,128)S(1)} collective-permute-done((f32[4,128,128]{2,1,0:T(8,128)}, f32[4,128,128]{2,1,0:T(8,128)S(1)}, u32[]{:S(2)}, u32[]{:S(2)}) %collective-permute-start) | collective-permute-done | bytes 262176 | tf_op jit(solution)/shard_map/while/body/eval_jaxpr/ppermute | solution.py:14
  321.7 9.9 %collective-permute-done = f32[4,128,128]{2,1,0:T(8,128)S(1)} collective-permute-done((f32[4,128,128]{2,1,0:T(8,128)}, f32[4,128,128]{2,1,0:T(8,128)S(1)}, u32[]{:S(2)}, u32[]{:S(2)}) %collective-permute-start) | collective-permute-done | bytes 262176 | tf_op jit(solution)/shard_map/while/body/eval_jaxpr/ppermute | solution.py:14
  335.2 9.9 %collective-permute-done = f32[4,128,128]{2,1,0:T(8,128)S(1)} collective-permute-done((f32[4,128,128]{2,1,0:T(8,128)}, f32[4,128,128]{2,1,0:T(8,128)S(1)}, u32[]{:S(2)}, u32[]{:S(2)}) %collective-permute-start) | collective-permute-done | bytes 262176 | tf_op jit(solution)/shard_map/while/body/eval_jaxpr/ppermute | solution.py:14
  348.6 10.9 %collective-permute-done = f32[4,128,128]{2,1,0:T(8,128)S(1)} collective-permute-done((f32[4,128,128]{2,1,0:T(8,128)}, f32[4,128,128]{2,1,0:T(8,128)S(1)}, u32[]{:S(2)}, u32[]{:S(2)}) %collective-permute-start) | collective-permute-done | bytes 262176 | tf_op jit(solution)/shard_map/while/body/eval_jaxpr/ppermute | solution.py:14
  363.1 12.0 %collective-permute-done = f32[4,128,128]{2,1,0:T(8,128)S(1)} collective-permute-done((f32[4,128,128]{2,1,0:T(8,128)}, f32[4,128,128]{2,1,0:T(8,128)S(1)}, u32[]{:S(2)}, u32[]{:S(2)}) %collective-permute-start) | collective-permute-done | bytes 262176 | tf_op jit(solution)/shard_map/while/body/eval_jaxpr/ppermute | solution.py:14
  378.7 12.2 %collective-permute-done = f32[4,128,128]{2,1,0:T(8,128)S(1)} collective-permute-done((f32[4,128,128]{2,1,0:T(8,128)}, f32[4,128,128]{2,1,0:T(8,128)S(1)}, u32[]{:S(2)}, u32[]{:S(2)}) %collective-permute-start) | collective-permute-done | bytes 262176 | tf_op jit(solution)/shard_map/while/body/eval_jaxpr/ppermute | solution.py:14
  394.5 11.3 %collective-permute-done = f32[4,128,128]{2,1,0:T(8,128)S(1)} collective-permute-done((f32[4,128,128]{2,1,0:T(8,128)}, f32[4,128,128]{2,1,0:T(8,128)S(1)}, u32[]{:S(2)}, u32[]{:S(2)}) %collective-permute-start) | collective-permute-done | bytes 262176 | tf_op jit(solution)/shard_map/while/body/eval_jaxpr/ppermute | solution.py:14
  409.4 10.5 %collective-permute-done = f32[4,128,128]{2,1,0:T(8,128)S(1)} collective-permute-done((f32[4,128,128]{2,1,0:T(8,128)}, f32[4,128,128]{2,1,0:T(8,128)S(1)}, u32[]{:S(2)}, u32[]{:S(2)}) %collective-permute-start) | collective-permute-done | bytes 262176 | tf_op jit(solution)/shard_map/while/body/eval_jaxpr/ppermute | solution.py:14
  423.4 9.9 %collective-permute-done = f32[4,128,128]{2,1,0:T(8,128)S(1)} collective-permute-done((f32[4,128,128]{2,1,0:T(8,128)}, f32[4,128,128]{2,1,0:T(8,128)S(1)}, u32[]{:S(2)}, u32[]{:S(2)}) %collective-permute-start) | collective-permute-done | bytes 262176 | tf_op jit(solution)/shard_map/while/body/eval_jaxpr/ppermute | solution.py:14
  436.9 9.9 %collective-permute-done = f32[4,128,128]{2,1,0:T(8,128)S(1)} collective-permute-done((f32[4,128,128]{2,1,0:T(8,128)}, f32[4,128,128]{2,1,0:T(8,128)S(1)}, u32[]{:S(2)}, u32[]{:S(2)}) %collective-permute-start) | collective-permute-done | bytes 262176 | tf_op jit(solution)/shard_map/while/body/eval_jaxpr/ppermute | solution.py:14
  450.3 9.9 %collective-permute-done = f32[4,128,128]{2,1,0:T(8,128)S(1)} collective-permute-done((f32[4,128,128]{2,1,0:T(8,128)}, f32[4,128,128]{2,1,0:T(8,128)S(1)}, u32[]{:S(2)}, u32[]{:S(2)}) %collective-permute-start) | collective-permute-done | bytes 262176 | tf_op jit(solution)/shard_map/while/body/eval_jaxpr/ppermute | solution.py:14
  463.8 9.9 %collective-permute-done = f32[4,128,128]{2,1,0:T(8,128)S(1)} collective-permute-done((f32[4,128,128]{2,1,0:T(8,128)}, f32[4,128,128]{2,1,0:T(8,128)S(1)}, u32[]{:S(2)}, u32[]{:S(2)}) %collective-permute-start) | collective-permute-done | bytes 262176 | tf_op jit(solution)/shard_map/while/body/eval_jaxpr/ppermute | solution.py:14
  477.3 9.9 %collective-permute-done = f32[4,128,128]{2,1,0:T(8,128)S(1)} collective-permute-done((f32[4,128,128]{2,1,0:T(8,128)}, f32[4,128,128]{2,1,0:T(8,128)S(1)}, u32[]{:S(2)}, u32[]{:S(2)}) %collective-permute-start) | collective-permute-done | bytes 262176 | tf_op jit(solution)/shard_map/while/body/eval_jaxpr/ppermute | solution.py:14
  487.1 2.6 fusion.4
  489.8 4.1 multiply_reduce_fusion
  493.9 2.2 multiply_convert_fusion
  496.1 2.0 copy.8
  (73 shorter events, 99.3 us)
Async XLA Ops:
  6.5 34.4 %copy-start = (bf16[3072,512]{1,0:T(8,128)(2,1)S(1)}, bf16[3072,512]{1,0:T(8,128)(2,1)}, u32[]{:S(2)}) copy-start(bf16[3072,512]{1,0:T(8,128)(2,1)} %param.10) | copy-start | bytes 9437188
  6.5 34.4 %all-gather.2.cloned.1.call-start = ((), (), s32[]{:S(2)}) async-start(), calls=%async_computation | async-start | bytes 3538944 | tf_op jit(solution)/shard_map/all_gather | solution.py:20
  41.0 3.9 copy-start.3
  41.0 3.9 copy-start.5
  44.9 1.9 copy-start.4
  48.7 1.1 copy-start.1
  52.6 13.9 %collective-permute-start = (f32[4,128,128]{2,1,0:T(8,128)}, f32[4,128,128]{2,1,0:T(8,128)S(1)}, u32[]{:S(2)}, u32[]{:S(2)}) collective-permute-start(f32[4,128,128]{2,1,0:T(8,128)} %add.39), channel_id=1, source_target_pairs={{0,8},{8,16},{16,24},{24,32},{32,40},{40,48},{48,56},{56,64},{64,7... | collective-permute-start | bytes 786440 | tf_op jit(solution)/shard_map/while/body/eval_jaxpr/ppermute | solution.py:14
  68.1 13.0 %collective-permute-start = (f32[4,128,128]{2,1,0:T(8,128)}, f32[4,128,128]{2,1,0:T(8,128)S(1)}, u32[]{:S(2)}, u32[]{:S(2)}) collective-permute-start(f32[4,128,128]{2,1,0:T(8,128)} %add.39), channel_id=1, source_target_pairs={{0,8},{8,16},{16,24},{24,32},{32,40},{40,48},{48,56},{56,64},{64,7... | collective-permute-start | bytes 786440 | tf_op jit(solution)/shard_map/while/body/eval_jaxpr/ppermute | solution.py:14
  82.8 12.1 %collective-permute-start = (f32[4,128,128]{2,1,0:T(8,128)}, f32[4,128,128]{2,1,0:T(8,128)S(1)}, u32[]{:S(2)}, u32[]{:S(2)}) collective-permute-start(f32[4,128,128]{2,1,0:T(8,128)} %add.39), channel_id=1, source_target_pairs={{0,8},{8,16},{16,24},{24,32},{32,40},{40,48},{48,56},{56,64},{64,7... | collective-permute-start | bytes 786440 | tf_op jit(solution)/shard_map/while/body/eval_jaxpr/ppermute | solution.py:14
  96.6 11.8 %collective-permute-start = (f32[4,128,128]{2,1,0:T(8,128)}, f32[4,128,128]{2,1,0:T(8,128)S(1)}, u32[]{:S(2)}, u32[]{:S(2)}) collective-permute-start(f32[4,128,128]{2,1,0:T(8,128)} %add.39), channel_id=1, source_target_pairs={{0,8},{8,16},{16,24},{24,32},{32,40},{40,48},{48,56},{56,64},{64,7... | collective-permute-start | bytes 786440 | tf_op jit(solution)/shard_map/while/body/eval_jaxpr/ppermute | solution.py:14
  110.1 11.8 %collective-permute-start = (f32[4,128,128]{2,1,0:T(8,128)}, f32[4,128,128]{2,1,0:T(8,128)S(1)}, u32[]{:S(2)}, u32[]{:S(2)}) collective-permute-start(f32[4,128,128]{2,1,0:T(8,128)} %add.39), channel_id=1, source_target_pairs={{0,8},{8,16},{16,24},{24,32},{32,40},{40,48},{48,56},{56,64},{64,7... | collective-permute-start | bytes 786440 | tf_op jit(solution)/shard_map/while/body/eval_jaxpr/ppermute | solution.py:14
  123.5 11.8 %collective-permute-start = (f32[4,128,128]{2,1,0:T(8,128)}, f32[4,128,128]{2,1,0:T(8,128)S(1)}, u32[]{:S(2)}, u32[]{:S(2)}) collective-permute-start(f32[4,128,128]{2,1,0:T(8,128)} %add.39), channel_id=1, source_target_pairs={{0,8},{8,16},{16,24},{24,32},{32,40},{40,48},{48,56},{56,64},{64,7... | collective-permute-start | bytes 786440 | tf_op jit(solution)/shard_map/while/body/eval_jaxpr/ppermute | solution.py:14
  137.0 11.8 %collective-permute-start = (f32[4,128,128]{2,1,0:T(8,128)}, f32[4,128,128]{2,1,0:T(8,128)S(1)}, u32[]{:S(2)}, u32[]{:S(2)}) collective-permute-start(f32[4,128,128]{2,1,0:T(8,128)} %add.39), channel_id=1, source_target_pairs={{0,8},{8,16},{16,24},{24,32},{32,40},{40,48},{48,56},{56,64},{64,7... | collective-permute-start | bytes 786440 | tf_op jit(solution)/shard_map/while/body/eval_jaxpr/ppermute | solution.py:14
  150.4 11.8 %collective-permute-start = (f32[4,128,128]{2,1,0:T(8,128)}, f32[4,128,128]{2,1,0:T(8,128)S(1)}, u32[]{:S(2)}, u32[]{:S(2)}) collective-permute-start(f32[4,128,128]{2,1,0:T(8,128)} %add.39), channel_id=1, source_target_pairs={{0,8},{8,16},{16,24},{24,32},{32,40},{40,48},{48,56},{56,64},{64,7... | collective-permute-start | bytes 786440 | tf_op jit(solution)/shard_map/while/body/eval_jaxpr/ppermute | solution.py:14
  163.9 11.8 %collective-permute-start = (f32[4,128,128]{2,1,0:T(8,128)}, f32[4,128,128]{2,1,0:T(8,128)S(1)}, u32[]{:S(2)}, u32[]{:S(2)}) collective-permute-start(f32[4,128,128]{2,1,0:T(8,128)} %add.39), channel_id=1, source_target_pairs={{0,8},{8,16},{16,24},{24,32},{32,40},{40,48},{48,56},{56,64},{64,7... | collective-permute-start | bytes 786440 | tf_op jit(solution)/shard_map/while/body/eval_jaxpr/ppermute | solution.py:14
  177.3 12.5 %collective-permute-start = (f32[4,128,128]{2,1,0:T(8,128)}, f32[4,128,128]{2,1,0:T(8,128)S(1)}, u32[]{:S(2)}, u32[]{:S(2)}) collective-permute-start(f32[4,128,128]{2,1,0:T(8,128)} %add.39), channel_id=1, source_target_pairs={{0,8},{8,16},{16,24},{24,32},{32,40},{40,48},{48,56},{56,64},{64,7... | collective-permute-start | bytes 786440 | tf_op jit(solution)/shard_map/while/body/eval_jaxpr/ppermute | solution.py:14
  191.5 13.6 %collective-permute-start = (f32[4,128,128]{2,1,0:T(8,128)}, f32[4,128,128]{2,1,0:T(8,128)S(1)}, u32[]{:S(2)}, u32[]{:S(2)}) collective-permute-start(f32[4,128,128]{2,1,0:T(8,128)} %add.39), channel_id=1, source_target_pairs={{0,8},{8,16},{16,24},{24,32},{32,40},{40,48},{48,56},{56,64},{64,7... | collective-permute-start | bytes 786440 | tf_op jit(solution)/shard_map/while/body/eval_jaxpr/ppermute | solution.py:14
  206.8 14.4 %collective-permute-start = (f32[4,128,128]{2,1,0:T(8,128)}, f32[4,128,128]{2,1,0:T(8,128)S(1)}, u32[]{:S(2)}, u32[]{:S(2)}) collective-permute-start(f32[4,128,128]{2,1,0:T(8,128)} %add.39), channel_id=1, source_target_pairs={{0,8},{8,16},{16,24},{24,32},{32,40},{40,48},{48,56},{56,64},{64,7... | collective-permute-start | bytes 786440 | tf_op jit(solution)/shard_map/while/body/eval_jaxpr/ppermute | solution.py:14
  222.9 13.6 %collective-permute-start = (f32[4,128,128]{2,1,0:T(8,128)}, f32[4,128,128]{2,1,0:T(8,128)S(1)}, u32[]{:S(2)}, u32[]{:S(2)}) collective-permute-start(f32[4,128,128]{2,1,0:T(8,128)} %add.39), channel_id=1, source_target_pairs={{0,8},{8,16},{16,24},{24,32},{32,40},{40,48},{48,56},{56,64},{64,7... | collective-permute-start | bytes 786440 | tf_op jit(solution)/shard_map/while/body/eval_jaxpr/ppermute | solution.py:14
  238.1 12.7 %collective-permute-start = (f32[4,128,128]{2,1,0:T(8,128)}, f32[4,128,128]{2,1,0:T(8,128)S(1)}, u32[]{:S(2)}, u32[]{:S(2)}) collective-permute-start(f32[4,128,128]{2,1,0:T(8,128)} %add.39), channel_id=1, source_target_pairs={{0,8},{8,16},{16,24},{24,32},{32,40},{40,48},{48,56},{56,64},{64,7... | collective-permute-start | bytes 786440 | tf_op jit(solution)/shard_map/while/body/eval_jaxpr/ppermute | solution.py:14
  252.5 11.8 %collective-permute-start = (f32[4,128,128]{2,1,0:T(8,128)}, f32[4,128,128]{2,1,0:T(8,128)S(1)}, u32[]{:S(2)}, u32[]{:S(2)}) collective-permute-start(f32[4,128,128]{2,1,0:T(8,128)} %add.39), channel_id=1, source_target_pairs={{0,8},{8,16},{16,24},{24,32},{32,40},{40,48},{48,56},{56,64},{64,7... | collective-permute-start | bytes 786440 | tf_op jit(solution)/shard_map/while/body/eval_jaxpr/ppermute | solution.py:14
  266.0 11.8 %collective-permute-start = (f32[4,128,128]{2,1,0:T(8,128)}, f32[4,128,128]{2,1,0:T(8,128)S(1)}, u32[]{:S(2)}, u32[]{:S(2)}) collective-permute-start(f32[4,128,128]{2,1,0:T(8,128)} %add.39), channel_id=1, source_target_pairs={{0,8},{8,16},{16,24},{24,32},{32,40},{40,48},{48,56},{56,64},{64,7... | collective-permute-start | bytes 786440 | tf_op jit(solution)/shard_map/while/body/eval_jaxpr/ppermute | solution.py:14
  279.4 11.8 %collective-permute-start = (f32[4,128,128]{2,1,0:T(8,128)}, f32[4,128,128]{2,1,0:T(8,128)S(1)}, u32[]{:S(2)}, u32[]{:S(2)}) collective-permute-start(f32[4,128,128]{2,1,0:T(8,128)} %add.39), channel_id=1, source_target_pairs={{0,8},{8,16},{16,24},{24,32},{32,40},{40,48},{48,56},{56,64},{64,7... | collective-permute-start | bytes 786440 | tf_op jit(solution)/shard_map/while/body/eval_jaxpr/ppermute | solution.py:14
  292.9 11.8 %collective-permute-start = (f32[4,128,128]{2,1,0:T(8,128)}, f32[4,128,128]{2,1,0:T(8,128)S(1)}, u32[]{:S(2)}, u32[]{:S(2)}) collective-permute-start(f32[4,128,128]{2,1,0:T(8,128)} %add.39), channel_id=1, source_target_pairs={{0,8},{8,16},{16,24},{24,32},{32,40},{40,48},{48,56},{56,64},{64,7... | collective-permute-start | bytes 786440 | tf_op jit(solution)/shard_map/while/body/eval_jaxpr/ppermute | solution.py:14
  306.3 11.8 %collective-permute-start = (f32[4,128,128]{2,1,0:T(8,128)}, f32[4,128,128]{2,1,0:T(8,128)S(1)}, u32[]{:S(2)}, u32[]{:S(2)}) collective-permute-start(f32[4,128,128]{2,1,0:T(8,128)} %add.39), channel_id=1, source_target_pairs={{0,8},{8,16},{16,24},{24,32},{32,40},{40,48},{48,56},{56,64},{64,7... | collective-permute-start | bytes 786440 | tf_op jit(solution)/shard_map/while/body/eval_jaxpr/ppermute | solution.py:14
  319.8 11.8 %collective-permute-start = (f32[4,128,128]{2,1,0:T(8,128)}, f32[4,128,128]{2,1,0:T(8,128)S(1)}, u32[]{:S(2)}, u32[]{:S(2)}) collective-permute-start(f32[4,128,128]{2,1,0:T(8,128)} %add.39), channel_id=1, source_target_pairs={{0,8},{8,16},{16,24},{24,32},{32,40},{40,48},{48,56},{56,64},{64,7... | collective-permute-start | bytes 786440 | tf_op jit(solution)/shard_map/while/body/eval_jaxpr/ppermute | solution.py:14
  333.2 11.8 %collective-permute-start = (f32[4,128,128]{2,1,0:T(8,128)}, f32[4,128,128]{2,1,0:T(8,128)S(1)}, u32[]{:S(2)}, u32[]{:S(2)}) collective-permute-start(f32[4,128,128]{2,1,0:T(8,128)} %add.39), channel_id=1, source_target_pairs={{0,8},{8,16},{16,24},{24,32},{32,40},{40,48},{48,56},{56,64},{64,7... | collective-permute-start | bytes 786440 | tf_op jit(solution)/shard_map/while/body/eval_jaxpr/ppermute | solution.py:14
  346.7 12.8 %collective-permute-start = (f32[4,128,128]{2,1,0:T(8,128)}, f32[4,128,128]{2,1,0:T(8,128)S(1)}, u32[]{:S(2)}, u32[]{:S(2)}) collective-permute-start(f32[4,128,128]{2,1,0:T(8,128)} %add.39), channel_id=1, source_target_pairs={{0,8},{8,16},{16,24},{24,32},{32,40},{40,48},{48,56},{56,64},{64,7... | collective-permute-start | bytes 786440 | tf_op jit(solution)/shard_map/while/body/eval_jaxpr/ppermute | solution.py:14
  361.2 13.9 %collective-permute-start = (f32[4,128,128]{2,1,0:T(8,128)}, f32[4,128,128]{2,1,0:T(8,128)S(1)}, u32[]{:S(2)}, u32[]{:S(2)}) collective-permute-start(f32[4,128,128]{2,1,0:T(8,128)} %add.39), channel_id=1, source_target_pairs={{0,8},{8,16},{16,24},{24,32},{32,40},{40,48},{48,56},{56,64},{64,7... | collective-permute-start | bytes 786440 | tf_op jit(solution)/shard_map/while/body/eval_jaxpr/ppermute | solution.py:14
  376.8 14.1 %collective-permute-start = (f32[4,128,128]{2,1,0:T(8,128)}, f32[4,128,128]{2,1,0:T(8,128)S(1)}, u32[]{:S(2)}, u32[]{:S(2)}) collective-permute-start(f32[4,128,128]{2,1,0:T(8,128)} %add.39), channel_id=1, source_target_pairs={{0,8},{8,16},{16,24},{24,32},{32,40},{40,48},{48,56},{56,64},{64,7... | collective-permute-start | bytes 786440 | tf_op jit(solution)/shard_map/while/body/eval_jaxpr/ppermute | solution.py:14
  392.5 13.2 %collective-permute-start = (f32[4,128,128]{2,1,0:T(8,128)}, f32[4,128,128]{2,1,0:T(8,128)S(1)}, u32[]{:S(2)}, u32[]{:S(2)}) collective-permute-start(f32[4,128,128]{2,1,0:T(8,128)} %add.39), channel_id=1, source_target_pairs={{0,8},{8,16},{16,24},{24,32},{32,40},{40,48},{48,56},{56,64},{64,7... | collective-permute-start | bytes 786440 | tf_op jit(solution)/shard_map/while/body/eval_jaxpr/ppermute | solution.py:14
  407.5 12.4 %collective-permute-start = (f32[4,128,128]{2,1,0:T(8,128)}, f32[4,128,128]{2,1,0:T(8,128)S(1)}, u32[]{:S(2)}, u32[]{:S(2)}) collective-permute-start(f32[4,128,128]{2,1,0:T(8,128)} %add.39), channel_id=1, source_target_pairs={{0,8},{8,16},{16,24},{24,32},{32,40},{40,48},{48,56},{56,64},{64,7... | collective-permute-start | bytes 786440 | tf_op jit(solution)/shard_map/while/body/eval_jaxpr/ppermute | solution.py:14
  421.5 11.8 %collective-permute-start = (f32[4,128,128]{2,1,0:T(8,128)}, f32[4,128,128]{2,1,0:T(8,128)S(1)}, u32[]{:S(2)}, u32[]{:S(2)}) collective-permute-start(f32[4,128,128]{2,1,0:T(8,128)} %add.39), channel_id=1, source_target_pairs={{0,8},{8,16},{16,24},{24,32},{32,40},{40,48},{48,56},{56,64},{64,7... | collective-permute-start | bytes 786440 | tf_op jit(solution)/shard_map/while/body/eval_jaxpr/ppermute | solution.py:14
  435.0 11.8 %collective-permute-start = (f32[4,128,128]{2,1,0:T(8,128)}, f32[4,128,128]{2,1,0:T(8,128)S(1)}, u32[]{:S(2)}, u32[]{:S(2)}) collective-permute-start(f32[4,128,128]{2,1,0:T(8,128)} %add.39), channel_id=1, source_target_pairs={{0,8},{8,16},{16,24},{24,32},{32,40},{40,48},{48,56},{56,64},{64,7... | collective-permute-start | bytes 786440 | tf_op jit(solution)/shard_map/while/body/eval_jaxpr/ppermute | solution.py:14
  448.4 11.8 %collective-permute-start = (f32[4,128,128]{2,1,0:T(8,128)}, f32[4,128,128]{2,1,0:T(8,128)S(1)}, u32[]{:S(2)}, u32[]{:S(2)}) collective-permute-start(f32[4,128,128]{2,1,0:T(8,128)} %add.39), channel_id=1, source_target_pairs={{0,8},{8,16},{16,24},{24,32},{32,40},{40,48},{48,56},{56,64},{64,7... | collective-permute-start | bytes 786440 | tf_op jit(solution)/shard_map/while/body/eval_jaxpr/ppermute | solution.py:14
  461.9 11.8 %collective-permute-start = (f32[4,128,128]{2,1,0:T(8,128)}, f32[4,128,128]{2,1,0:T(8,128)S(1)}, u32[]{:S(2)}, u32[]{:S(2)}) collective-permute-start(f32[4,128,128]{2,1,0:T(8,128)} %add.39), channel_id=1, source_target_pairs={{0,8},{8,16},{16,24},{24,32},{32,40},{40,48},{48,56},{56,64},{64,7... | collective-permute-start | bytes 786440 | tf_op jit(solution)/shard_map/while/body/eval_jaxpr/ppermute | solution.py:14
  475.3 11.8 %collective-permute-start = (f32[4,128,128]{2,1,0:T(8,128)}, f32[4,128,128]{2,1,0:T(8,128)S(1)}, u32[]{:S(2)}, u32[]{:S(2)}) collective-permute-start(f32[4,128,128]{2,1,0:T(8,128)} %add.39), channel_id=1, source_target_pairs={{0,8},{8,16},{16,24},{24,32},{32,40},{40,48},{48,56},{56,64},{64,7... | collective-permute-start | bytes 786440 | tf_op jit(solution)/shard_map/while/body/eval_jaxpr/ppermute | solution.py:14
  489.8 4.2 copy-start.2
Sparse Core Ops, SparseCore 0:
  9.2 31.7 all-gather.1
where the time goes:
time: 507 us; the launch traced here: 505 us
  waiting for transfers between devices  357 us (70%)
  starting transfers between devices  60.6 us (12%)
  other arithmetic  54.9 us (11%)
  matrix products  15.3 us (3%)
  between operations  13.5 us (3%)
    ppermute x31, waiting for transfers between devices, from_behind(): return lax.ppermute(value, axis, pairs)  323 us
    ppermute x31, starting transfers between devices, from_behind(): return lax.ppermute(value, axis, pairs)  60.6 us
    add x31, other arithmetic, advance(): return from_behind(carried + local_state, 'ctx', 1)  51.8 us
    all_gather x1, waiting for transfers between devices, body(): piece_rows = lax.all_gather(tokens, 'tp', axis=0, tiled=True)  32.9 us
  transfers between devices with their start and end apart: 32, of which 32 were waited for; matrix products, arithmetic and copies ran while one was open for 0% of the time, Pallas kernels for 0%

commit v1 on v0

--- a/solution.py
+++ b/solution.py
@@ -17,7 +17,9 @@
 def body(tokens, w_query, w_key, w_value, norm_gain):
     local_width = w_query.shape[1]
     head_count = local_width // HEAD_DIM
-    piece_rows = lax.all_gather(tokens, "tp", axis=0, tiled=True)
+    piece_rows = jnp.concatenate(
+        lax.all_to_all(jnp.stack([tokens] * lax.axis_size("tp")), "tp", 0, 0), axis=0
+    )
     query_part = jnp.dot(piece_rows, w_query, preferred_element_type=jnp.float32).astype(
         jnp.bfloat16
     )

time: 507 us -> 508 us (level)
  between operations: 13.5 us -> 0.08 us
    all_to_all x0 -> x1, waiting for transfers between devices: none -> 37.7 us  [body(): lax.all_to_all(jnp.stack([tokens] * lax.axis_size('tp')), 'tp', 0, 0)]
    all_gather x1 -> x0, waiting for transfers between devices: 32.9 us -> none  [body(): piece_rows = lax.all_gather(tokens, 'tp', axis=0, tiled=True)]
where the time goes in v1:
time: 508 us; the launch traced here: 506 us
  waiting for transfers between devices  360 us (71%)
  starting transfers between devices  65.1 us (13%)
  other arithmetic  54.7 us (11%)
  matrix products  19.3 us (4%)
  local copies, waits for them, and re-layouts  6.43 us (1%)
    ppermute x31, waiting for transfers between devices, from_behind(): return lax.ppermute(value, axis, pairs)  322 us
    ppermute x31, starting transfers between devices, from_behind(): return lax.ppermute(value, axis, pairs)  60.6 us
    add x31, other arithmetic, advance(): return from_behind(carried + local_state, 'ctx', 1)  51.6 us
    all_to_all x1, waiting for transfers between devices, body(): lax.all_to_all(jnp.stack([tokens] * lax.axis_size('tp')), 'tp', 0, 0)  37.7 us
  transfers between devices with their start and end apart: 32, of which 32 were waited for; matrix products, arithmetic and copies ran while one was open for 0% of the time, Pallas kernels for 0%

profile of v1, /device:TPU:128, one launch (start us, length us, event | category | flops | bytes accessed | tf_op | source)
XLA Modules:
  0.0 505.9 jit_solution(10948354393140883473)
XLA Ops:
  0.0 3.2 stack.2
  3.2 4.5 all-to-all-start
  8.4 37.7 %all-to-all-done = bf16[8,64,3072]{2,1,0:T(8,128)(2,1)} async-done(((bf16[8,64,3072]{2,1,0:T(8,128)(2,1)}), bf16[8,64,3072]{2,1,0:T(8,128)(2,1)}, u32[]{:S(2)}, u32[]{:S(2)}) %all-to-all-start) | async-done | bytes 3145760 | tf_op jit(solution)/shard_map/all_to_all | solution.py:21
  46.2 3.9 convolution_convert_fusion
  50.1 3.9 convolution_convert_fusion.1
  54.0 3.8 convolution_convert_fusion.2
  60.1 434.8 %while.10 = (s32[]{:T(128)}, f32[4,128,128]{2,1,0:T(8,128)S(1)}, f32[4,128,128]{2,1,0:T(8,128)}, s32[]{:T(128)}) while((s32[]{:T(128)}, f32[4,128,128]{2,1,0:T(8,128)S(1)}, f32[4,128,128]{2,1,0:T(8,128)}, s32[]{:T(128)}) %tuple.19), condition=%wide.region_1.0_spmd, body=%wide.region_0.0_spmd.sunk | while | flops 65538 | bytes 1835101 | solution.py:46
  61.7 3.4 collective-permute-start
  65.1 9.8 %collective-permute-done = f32[4,128,128]{2,1,0:T(8,128)S(1)} collective-permute-done((f32[4,128,128]{2,1,0:T(8,128)}, f32[4,128,128]{2,1,0:T(8,128)S(1)}, u32[]{:S(2)}, u32[]{:S(2)}) %collective-permute-start) | collective-permute-done | bytes 262176 | tf_op jit(solution)/shard_map/while/body/eval_jaxpr/ppermute | solution.py:14
  76.6 1.9 collective-permute-start
  78.5 10.4 %collective-permute-done = f32[4,128,128]{2,1,0:T(8,128)S(1)} collective-permute-done((f32[4,128,128]{2,1,0:T(8,128)}, f32[4,128,128]{2,1,0:T(8,128)S(1)}, u32[]{:S(2)}, u32[]{:S(2)}) %collective-permute-start) | collective-permute-done | bytes 262176 | tf_op jit(solution)/shard_map/while/body/eval_jaxpr/ppermute | solution.py:14
  92.5 9.9 %collective-permute-done = f32[4,128,128]{2,1,0:T(8,128)S(1)} collective-permute-done((f32[4,128,128]{2,1,0:T(8,128)}, f32[4,128,128]{2,1,0:T(8,128)S(1)}, u32[]{:S(2)}, u32[]{:S(2)}) %collective-permute-start) | collective-permute-done | bytes 262176 | tf_op jit(solution)/shard_map/while/body/eval_jaxpr/ppermute | solution.py:14
  104.0 1.9 collective-permute-start
  105.9 9.9 %collective-permute-done = f32[4,128,128]{2,1,0:T(8,128)S(1)} collective-permute-done((f32[4,128,128]{2,1,0:T(8,128)}, f32[4,128,128]{2,1,0:T(8,128)S(1)}, u32[]{:S(2)}, u32[]{:S(2)}) %collective-permute-start) | collective-permute-done | bytes 262176 | tf_op jit(solution)/shard_map/while/body/eval_jaxpr/ppermute | solution.py:14
  117.5 1.9 collective-permute-start
  119.4 9.9 %collective-permute-done = f32[4,128,128]{2,1,0:T(8,128)S(1)} collective-permute-done((f32[4,128,128]{2,1,0:T(8,128)}, f32[4,128,128]{2,1,0:T(8,128)S(1)}, u32[]{:S(2)}, u32[]{:S(2)}) %collective-permute-start) | collective-permute-done | bytes 262176 | tf_op jit(solution)/shard_map/while/body/eval_jaxpr/ppermute | solution.py:14
  132.8 9.9 %collective-permute-done = f32[4,128,128]{2,1,0:T(8,128)S(1)} collective-permute-done((f32[4,128,128]{2,1,0:T(8,128)}, f32[4,128,128]{2,1,0:T(8,128)S(1)}, u32[]{:S(2)}, u32[]{:S(2)}) %collective-permute-start) | collective-permute-done | bytes 262176 | tf_op jit(solution)/shard_map/while/body/eval_jaxpr/ppermute | solution.py:14
  144.3 1.9 collective-permute-start
  146.3 9.9 %collective-permute-done = f32[4,128,128]{2,1,0:T(8,128)S(1)} collective-permute-done((f32[4,128,128]{2,1,0:T(8,128)}, f32[4,128,128]{2,1,0:T(8,128)S(1)}, u32[]{:S(2)}, u32[]{:S(2)}) %collective-permute-start) | collective-permute-done | bytes 262176 | tf_op jit(solution)/shard_map/while/body/eval_jaxpr/ppermute | solution.py:14
  157.8 1.9 collective-permute-start
  159.7 9.9 %collective-permute-done = f32[4,128,128]{2,1,0:T(8,128)S(1)} collective-permute-done((f32[4,128,128]{2,1,0:T(8,128)}, f32[4,128,128]{2,1,0:T(8,128)S(1)}, u32[]{:S(2)}, u32[]{:S(2)}) %collective-permute-start) | collective-permute-done | bytes 262176 | tf_op jit(solution)/shard_map/while/body/eval_jaxpr/ppermute | solution.py:14
  173.2 10.4 %collective-permute-done = f32[4,128,128]{2,1,0:T(8,128)S(1)} collective-permute-done((f32[4,128,128]{2,1,0:T(8,128)}, f32[4,128,128]{2,1,0:T(8,128)S(1)}, u32[]{:S(2)}, u32[]{:S(2)}) %collective-permute-start) | collective-permute-done | bytes 262176 | tf_op jit(solution)/shard_map/while/body/eval_jaxpr/ppermute | solution.py:14
  187.2 11.5 %collective-permute-done = f32[4,128,128]{2,1,0:T(8,128)S(1)} collective-permute-done((f32[4,128,128]{2,1,0:T(8,128)}, f32[4,128,128]{2,1,0:T(8,128)S(1)}, u32[]{:S(2)}, u32[]{:S(2)}) %collective-permute-start) | collective-permute-done | bytes 262176 | tf_op jit(solution)/shard_map/while/body/eval_jaxpr/ppermute | solution.py:14
  202.3 12.6 %collective-permute-done = f32[4,128,128]{2,1,0:T(8,128)S(1)} collective-permute-done((f32[4,128,128]{2,1,0:T(8,128)}, f32[4,128,128]{2,1,0:T(8,128)S(1)}, u32[]{:S(2)}, u32[]{:S(2)}) %collective-permute-start) | collective-permute-done | bytes 262176 | tf_op jit(solution)/shard_map/while/body/eval_jaxpr/ppermute | solution.py:14
  218.5 11.8 %collective-permute-done = f32[4,128,128]{2,1,0:T(8,128)S(1)} collective-permute-done((f32[4,128,128]{2,1,0:T(8,128)}, f32[4,128,128]{2,1,0:T(8,128)S(1)}, u32[]{:S(2)}, u32[]{:S(2)}) %collective-permute-start) | collective-permute-done | bytes 262176 | tf_op jit(solution)/shard_map/while/body/eval_jaxpr/ppermute | solution.py:14
  233.9 10.9 %collective-permute-done = f32[4,128,128]{2,1,0:T(8,128)S(1)} collective-permute-done((f32[4,128,128]{2,1,0:T(8,128)}, f32[4,128,128]{2,1,0:T(8,128)S(1)}, u32[]{:S(2)}, u32[]{:S(2)}) %collective-permute-start) | collective-permute-done | bytes 262176 | tf_op jit(solution)/shard_map/while/body/eval_jaxpr/ppermute | solution.py:14
  248.4 10.1 %collective-permute-done = f32[4,128,128]{2,1,0:T(8,128)S(1)} collective-permute-done((f32[4,128,128]{2,1,0:T(8,128)}, f32[4,128,128]{2,1,0:T(8,128)S(1)}, u32[]{:S(2)}, u32[]{:S(2)}) %collective-permute-start) | collective-permute-done | bytes 262176 | tf_op jit(solution)/shard_map/while/body/eval_jaxpr/ppermute | solution.py:14
  262.1 9.9 %collective-permute-done = f32[4,128,128]{2,1,0:T(8,128)S(1)} collective-permute-done((f32[4,128,128]{2,1,0:T(8,128)}, f32[4,128,128]{2,1,0:T(8,128)S(1)}, u32[]{:S(2)}, u32[]{:S(2)}) %collective-permute-start) | collective-permute-done | bytes 262176 | tf_op jit(solution)/shard_map/while/body/eval_jaxpr/ppermute | solution.py:14
  275.5 9.9 %collective-permute-done = f32[4,128,128]{2,1,0:T(8,128)S(1)} collective-permute-done((f32[4,128,128]{2,1,0:T(8,128)}, f32[4,128,128]{2,1,0:T(8,128)S(1)}, u32[]{:S(2)}, u32[]{:S(2)}) %collective-permute-start) | collective-permute-done | bytes 262176 | tf_op jit(solution)/shard_map/while/body/eval_jaxpr/ppermute | solution.py:14
  289.0 9.9 %collective-permute-done = f32[4,128,128]{2,1,0:T(8,128)S(1)} collective-permute-done((f32[4,128,128]{2,1,0:T(8,128)}, f32[4,128,128]{2,1,0:T(8,128)S(1)}, u32[]{:S(2)}, u32[]{:S(2)}) %collective-permute-start) | collective-permute-done | bytes 262176 | tf_op jit(solution)/shard_map/while/body/eval_jaxpr/ppermute | solution.py:14
  302.4 9.9 %collective-permute-done = f32[4,128,128]{2,1,0:T(8,128)S(1)} collective-permute-done((f32[4,128,128]{2,1,0:T(8,128)}, f32[4,128,128]{2,1,0:T(8,128)S(1)}, u32[]{:S(2)}, u32[]{:S(2)}) %collective-permute-start) | collective-permute-done | bytes 262176 | tf_op jit(solution)/shard_map/while/body/eval_jaxpr/ppermute | solution.py:14
  315.9 9.9 %collective-permute-done = f32[4,128,128]{2,1,0:T(8,128)S(1)} collective-permute-done((f32[4,128,128]{2,1,0:T(8,128)}, f32[4,128,128]{2,1,0:T(8,128)S(1)}, u32[]{:S(2)}, u32[]{:S(2)}) %collective-permute-start) | collective-permute-done | bytes 262176 | tf_op jit(solution)/shard_map/while/body/eval_jaxpr/ppermute | solution.py:14
  329.3 9.9 %collective-permute-done = f32[4,128,128]{2,1,0:T(8,128)S(1)} collective-permute-done((f32[4,128,128]{2,1,0:T(8,128)}, f32[4,128,128]{2,1,0:T(8,128)S(1)}, u32[]{:S(2)}, u32[]{:S(2)}) %collective-permute-start) | collective-permute-done | bytes 262176 | tf_op jit(solution)/shard_map/while/body/eval_jaxpr/ppermute | solution.py:14
  342.8 10.7 %collective-permute-done = f32[4,128,128]{2,1,0:T(8,128)S(1)} collective-permute-done((f32[4,128,128]{2,1,0:T(8,128)}, f32[4,128,128]{2,1,0:T(8,128)S(1)}, u32[]{:S(2)}, u32[]{:S(2)}) %collective-permute-start) | collective-permute-done | bytes 262176 | tf_op jit(solution)/shard_map/while/body/eval_jaxpr/ppermute | solution.py:14
  357.1 11.9 %collective-permute-done = f32[4,128,128]{2,1,0:T(8,128)S(1)} collective-permute-done((f32[4,128,128]{2,1,0:T(8,128)}, f32[4,128,128]{2,1,0:T(8,128)S(1)}, u32[]{:S(2)}, u32[]{:S(2)}) %collective-permute-start) | collective-permute-done | bytes 262176 | tf_op jit(solution)/shard_map/while/body/eval_jaxpr/ppermute | solution.py:14
  372.5 12.3 %collective-permute-done = f32[4,128,128]{2,1,0:T(8,128)S(1)} collective-permute-done((f32[4,128,128]{2,1,0:T(8,128)}, f32[4,128,128]{2,1,0:T(8,128)S(1)}, u32[]{:S(2)}, u32[]{:S(2)}) %collective-permute-start) | collective-permute-done | bytes 262176 | tf_op jit(solution)/shard_map/while/body/eval_jaxpr/ppermute | solution.py:14
  388.4 11.5 %collective-permute-done = f32[4,128,128]{2,1,0:T(8,128)S(1)} collective-permute-done((f32[4,128,128]{2,1,0:T(8,128)}, f32[4,128,128]{2,1,0:T(8,128)S(1)}, u32[]{:S(2)}, u32[]{:S(2)}) %collective-permute-start) | collective-permute-done | bytes 262176 | tf_op jit(solution)/shard_map/while/body/eval_jaxpr/ppermute | solution.py:14
  403.5 10.6 %collective-permute-done = f32[4,128,128]{2,1,0:T(8,128)S(1)} collective-permute-done((f32[4,128,128]{2,1,0:T(8,128)}, f32[4,128,128]{2,1,0:T(8,128)S(1)}, u32[]{:S(2)}, u32[]{:S(2)}) %collective-permute-start) | collective-permute-done | bytes 262176 | tf_op jit(solution)/shard_map/while/body/eval_jaxpr/ppermute | solution.py:14
  417.7 9.9 %collective-permute-done = f32[4,128,128]{2,1,0:T(8,128)S(1)} collective-permute-done((f32[4,128,128]{2,1,0:T(8,128)}, f32[4,128,128]{2,1,0:T(8,128)S(1)}, u32[]{:S(2)}, u32[]{:S(2)}) %collective-permute-start) | collective-permute-done | bytes 262176 | tf_op jit(solution)/shard_map/while/body/eval_jaxpr/ppermute | solution.py:14
  431.2 9.9 %collective-permute-done = f32[4,128,128]{2,1,0:T(8,128)S(1)} collective-permute-done((f32[4,128,128]{2,1,0:T(8,128)}, f32[4,128,128]{2,1,0:T(8,128)S(1)}, u32[]{:S(2)}, u32[]{:S(2)}) %collective-permute-start) | collective-permute-done | bytes 262176 | tf_op jit(solution)/shard_map/while/body/eval_jaxpr/ppermute | solution.py:14
  444.6 9.9 %collective-permute-done = f32[4,128,128]{2,1,0:T(8,128)S(1)} collective-permute-done((f32[4,128,128]{2,1,0:T(8,128)}, f32[4,128,128]{2,1,0:T(8,128)S(1)}, u32[]{:S(2)}, u32[]{:S(2)}) %collective-permute-start) | collective-permute-done | bytes 262176 | tf_op jit(solution)/shard_map/while/body/eval_jaxpr/ppermute | solution.py:14
  458.1 9.9 %collective-permute-done = f32[4,128,128]{2,1,0:T(8,128)S(1)} collective-permute-done((f32[4,128,128]{2,1,0:T(8,128)}, f32[4,128,128]{2,1,0:T(8,128)S(1)}, u32[]{:S(2)}, u32[]{:S(2)}) %collective-permute-start) | collective-permute-done | bytes 262176 | tf_op jit(solution)/shard_map/while/body/eval_jaxpr/ppermute | solution.py:14
  471.5 9.9 %collective-permute-done = f32[4,128,128]{2,1,0:T(8,128)S(1)} collective-permute-done((f32[4,128,128]{2,1,0:T(8,128)}, f32[4,128,128]{2,1,0:T(8,128)S(1)}, u32[]{:S(2)}, u32[]{:S(2)}) %collective-permute-start) | collective-permute-done | bytes 262176 | tf_op jit(solution)/shard_map/while/body/eval_jaxpr/ppermute | solution.py:14
  485.0 9.9 %collective-permute-done = f32[4,128,128]{2,1,0:T(8,128)S(1)} collective-permute-done((f32[4,128,128]{2,1,0:T(8,128)}, f32[4,128,128]{2,1,0:T(8,128)S(1)}, u32[]{:S(2)}, u32[]{:S(2)}) %collective-permute-start) | collective-permute-done | bytes 262176 | tf_op jit(solution)/shard_map/while/body/eval_jaxpr/ppermute | solution.py:14
  494.8 2.6 fusion.4
  497.5 4.2 multiply_reduce_fusion
  501.7 2.2 multiply_convert_fusion
  503.8 2.0 copy.8
  (71 shorter events, 102.4 us)
Async XLA Ops:
  0.0 46.2 %copy-start = (bf16[3072,512]{1,0:T(8,128)(2,1)S(1)}, bf16[3072,512]{1,0:T(8,128)(2,1)}, u32[]{:S(2)}) copy-start(bf16[3072,512]{1,0:T(8,128)(2,1)} %param.10) | copy-start | bytes 9437188
  3.2 43.0 %all-to-all-start = ((bf16[8,64,3072]{2,1,0:T(8,128)(2,1)}), bf16[8,64,3072]{2,1,0:T(8,128)(2,1)}, u32[]{:S(2)}, u32[]{:S(2)}) async-start(bf16[8,64,3072]{2,1,0:T(8,128)(2,1)} %stack.2), calls=%async_computation | async-start | bytes 6291456 | tf_op jit(solution)/shard_map/all_to_all | solution.py:21
  46.2 3.9 copy-start.3
  50.1 3.9 copy-start.4
  57.9 1.1 copy-start.1
  61.7 13.2 %collective-permute-start = (f32[4,128,128]{2,1,0:T(8,128)}, f32[4,128,128]{2,1,0:T(8,128)S(1)}, u32[]{:S(2)}, u32[]{:S(2)}) collective-permute-start(f32[4,128,128]{2,1,0:T(8,128)} %add.39), channel_id=1, source_target_pairs={{0,8},{8,16},{16,24},{24,32},{32,40},{40,48},{48,56},{56,64},{64,7... | collective-permute-start | bytes 786440 | tf_op jit(solution)/shard_map/while/body/eval_jaxpr/ppermute | solution.py:14
  76.6 12.3 %collective-permute-start = (f32[4,128,128]{2,1,0:T(8,128)}, f32[4,128,128]{2,1,0:T(8,128)S(1)}, u32[]{:S(2)}, u32[]{:S(2)}) collective-permute-start(f32[4,128,128]{2,1,0:T(8,128)} %add.39), channel_id=1, source_target_pairs={{0,8},{8,16},{16,24},{24,32},{32,40},{40,48},{48,56},{56,64},{64,7... | collective-permute-start | bytes 786440 | tf_op jit(solution)/shard_map/while/body/eval_jaxpr/ppermute | solution.py:14
  90.6 11.8 %collective-permute-start = (f32[4,128,128]{2,1,0:T(8,128)}, f32[4,128,128]{2,1,0:T(8,128)S(1)}, u32[]{:S(2)}, u32[]{:S(2)}) collective-permute-start(f32[4,128,128]{2,1,0:T(8,128)} %add.39), channel_id=1, source_target_pairs={{0,8},{8,16},{16,24},{24,32},{32,40},{40,48},{48,56},{56,64},{64,7... | collective-permute-start | bytes 786440 | tf_op jit(solution)/shard_map/while/body/eval_jaxpr/ppermute | solution.py:14
  104.0 11.8 %collective-permute-start = (f32[4,128,128]{2,1,0:T(8,128)}, f32[4,128,128]{2,1,0:T(8,128)S(1)}, u32[]{:S(2)}, u32[]{:S(2)}) collective-permute-start(f32[4,128,128]{2,1,0:T(8,128)} %add.39), channel_id=1, source_target_pairs={{0,8},{8,16},{16,24},{24,32},{32,40},{40,48},{48,56},{56,64},{64,7... | collective-permute-start | bytes 786440 | tf_op jit(solution)/shard_map/while/body/eval_jaxpr/ppermute | solution.py:14
  117.5 11.8 %collective-permute-start = (f32[4,128,128]{2,1,0:T(8,128)}, f32[4,128,128]{2,1,0:T(8,128)S(1)}, u32[]{:S(2)}, u32[]{:S(2)}) collective-permute-start(f32[4,128,128]{2,1,0:T(8,128)} %add.39), channel_id=1, source_target_pairs={{0,8},{8,16},{16,24},{24,32},{32,40},{40,48},{48,56},{56,64},{64,7... | collective-permute-start | bytes 786440 | tf_op jit(solution)/shard_map/while/body/eval_jaxpr/ppermute | solution.py:14
  130.9 11.8 %collective-permute-start = (f32[4,128,128]{2,1,0:T(8,128)}, f32[4,128,128]{2,1,0:T(8,128)S(1)}, u32[]{:S(2)}, u32[]{:S(2)}) collective-permute-start(f32[4,128,128]{2,1,0:T(8,128)} %add.39), channel_id=1, source_target_pairs={{0,8},{8,16},{16,24},{24,32},{32,40},{40,48},{48,56},{56,64},{64,7... | collective-permute-start | bytes 786440 | tf_op jit(solution)/shard_map/while/body/eval_jaxpr/ppermute | solution.py:14
  144.3 11.8 %collective-permute-start = (f32[4,128,128]{2,1,0:T(8,128)}, f32[4,128,128]{2,1,0:T(8,128)S(1)}, u32[]{:S(2)}, u32[]{:S(2)}) collective-permute-start(f32[4,128,128]{2,1,0:T(8,128)} %add.39), channel_id=1, source_target_pairs={{0,8},{8,16},{16,24},{24,32},{32,40},{40,48},{48,56},{56,64},{64,7... | collective-permute-start | bytes 786440 | tf_op jit(solution)/shard_map/while/body/eval_jaxpr/ppermute | solution.py:14
  157.8 11.8 %collective-permute-start = (f32[4,128,128]{2,1,0:T(8,128)}, f32[4,128,128]{2,1,0:T(8,128)S(1)}, u32[]{:S(2)}, u32[]{:S(2)}) collective-permute-start(f32[4,128,128]{2,1,0:T(8,128)} %add.39), channel_id=1, source_target_pairs={{0,8},{8,16},{16,24},{24,32},{32,40},{40,48},{48,56},{56,64},{64,7... | collective-permute-start | bytes 786440 | tf_op jit(solution)/shard_map/while/body/eval_jaxpr/ppermute | solution.py:14
  171.2 12.3 %collective-permute-start = (f32[4,128,128]{2,1,0:T(8,128)}, f32[4,128,128]{2,1,0:T(8,128)S(1)}, u32[]{:S(2)}, u32[]{:S(2)}) collective-permute-start(f32[4,128,128]{2,1,0:T(8,128)} %add.39), channel_id=1, source_target_pairs={{0,8},{8,16},{16,24},{24,32},{32,40},{40,48},{48,56},{56,64},{64,7... | collective-permute-start | bytes 786440 | tf_op jit(solution)/shard_map/while/body/eval_jaxpr/ppermute | solution.py:14
  185.2 13.5 %collective-permute-start = (f32[4,128,128]{2,1,0:T(8,128)}, f32[4,128,128]{2,1,0:T(8,128)S(1)}, u32[]{:S(2)}, u32[]{:S(2)}) collective-permute-start(f32[4,128,128]{2,1,0:T(8,128)} %add.39), channel_id=1, source_target_pairs={{0,8},{8,16},{16,24},{24,32},{32,40},{40,48},{48,56},{56,64},{64,7... | collective-permute-start | bytes 786440 | tf_op jit(solution)/shard_map/while/body/eval_jaxpr/ppermute | solution.py:14
  200.4 14.6 %collective-permute-start = (f32[4,128,128]{2,1,0:T(8,128)}, f32[4,128,128]{2,1,0:T(8,128)S(1)}, u32[]{:S(2)}, u32[]{:S(2)}) collective-permute-start(f32[4,128,128]{2,1,0:T(8,128)} %add.39), channel_id=1, source_target_pairs={{0,8},{8,16},{16,24},{24,32},{32,40},{40,48},{48,56},{56,64},{64,7... | collective-permute-start | bytes 786440 | tf_op jit(solution)/shard_map/while/body/eval_jaxpr/ppermute | solution.py:14
  216.6 13.7 %collective-permute-start = (f32[4,128,128]{2,1,0:T(8,128)}, f32[4,128,128]{2,1,0:T(8,128)S(1)}, u32[]{:S(2)}, u32[]{:S(2)}) collective-permute-start(f32[4,128,128]{2,1,0:T(8,128)} %add.39), channel_id=1, source_target_pairs={{0,8},{8,16},{16,24},{24,32},{32,40},{40,48},{48,56},{56,64},{64,7... | collective-permute-start | bytes 786440 | tf_op jit(solution)/shard_map/while/body/eval_jaxpr/ppermute | solution.py:14
  232.0 12.9 %collective-permute-start = (f32[4,128,128]{2,1,0:T(8,128)}, f32[4,128,128]{2,1,0:T(8,128)S(1)}, u32[]{:S(2)}, u32[]{:S(2)}) collective-permute-start(f32[4,128,128]{2,1,0:T(8,128)} %add.39), channel_id=1, source_target_pairs={{0,8},{8,16},{16,24},{24,32},{32,40},{40,48},{48,56},{56,64},{64,7... | collective-permute-start | bytes 786440 | tf_op jit(solution)/shard_map/while/body/eval_jaxpr/ppermute | solution.py:14
  246.5 12.0 %collective-permute-start = (f32[4,128,128]{2,1,0:T(8,128)}, f32[4,128,128]{2,1,0:T(8,128)S(1)}, u32[]{:S(2)}, u32[]{:S(2)}) collective-permute-start(f32[4,128,128]{2,1,0:T(8,128)} %add.39), channel_id=1, source_target_pairs={{0,8},{8,16},{16,24},{24,32},{32,40},{40,48},{48,56},{56,64},{64,7... | collective-permute-start | bytes 786440 | tf_op jit(solution)/shard_map/while/body/eval_jaxpr/ppermute | solution.py:14
  260.2 11.8 %collective-permute-start = (f32[4,128,128]{2,1,0:T(8,128)}, f32[4,128,128]{2,1,0:T(8,128)S(1)}, u32[]{:S(2)}, u32[]{:S(2)}) collective-permute-start(f32[4,128,128]{2,1,0:T(8,128)} %add.39), channel_id=1, source_target_pairs={{0,8},{8,16},{16,24},{24,32},{32,40},{40,48},{48,56},{56,64},{64,7... | collective-permute-start | bytes 786440 | tf_op jit(solution)/shard_map/while/body/eval_jaxpr/ppermute | solution.py:14
  273.6 11.8 %collective-permute-start = (f32[4,128,128]{2,1,0:T(8,128)}, f32[4,128,128]{2,1,0:T(8,128)S(1)}, u32[]{:S(2)}, u32[]{:S(2)}) collective-permute-start(f32[4,128,128]{2,1,0:T(8,128)} %add.39), channel_id=1, source_target_pairs={{0,8},{8,16},{16,24},{24,32},{32,40},{40,48},{48,56},{56,64},{64,7... | collective-permute-start | bytes 786440 | tf_op jit(solution)/shard_map/while/body/eval_jaxpr/ppermute | solution.py:14
  287.1 11.8 %collective-permute-start = (f32[4,128,128]{2,1,0:T(8,128)}, f32[4,128,128]{2,1,0:T(8,128)S(1)}, u32[]{:S(2)}, u32[]{:S(2)}) collective-permute-start(f32[4,128,128]{2,1,0:T(8,128)} %add.39), channel_id=1, source_target_pairs={{0,8},{8,16},{16,24},{24,32},{32,40},{40,48},{48,56},{56,64},{64,7... | collective-permute-start | bytes 786440 | tf_op jit(solution)/shard_map/while/body/eval_jaxpr/ppermute | solution.py:14
  300.5 11.8 %collective-permute-start = (f32[4,128,128]{2,1,0:T(8,128)}, f32[4,128,128]{2,1,0:T(8,128)S(1)}, u32[]{:S(2)}, u32[]{:S(2)}) collective-permute-start(f32[4,128,128]{2,1,0:T(8,128)} %add.39), channel_id=1, source_target_pairs={{0,8},{8,16},{16,24},{24,32},{32,40},{40,48},{48,56},{56,64},{64,7... | collective-permute-start | bytes 786440 | tf_op jit(solution)/shard_map/while/body/eval_jaxpr/ppermute | solution.py:14
  314.0 11.8 %collective-permute-start = (f32[4,128,128]{2,1,0:T(8,128)}, f32[4,128,128]{2,1,0:T(8,128)S(1)}, u32[]{:S(2)}, u32[]{:S(2)}) collective-permute-start(f32[4,128,128]{2,1,0:T(8,128)} %add.39), channel_id=1, source_target_pairs={{0,8},{8,16},{16,24},{24,32},{32,40},{40,48},{48,56},{56,64},{64,7... | collective-permute-start | bytes 786440 | tf_op jit(solution)/shard_map/while/body/eval_jaxpr/ppermute | solution.py:14
  327.4 11.8 %collective-permute-start = (f32[4,128,128]{2,1,0:T(8,128)}, f32[4,128,128]{2,1,0:T(8,128)S(1)}, u32[]{:S(2)}, u32[]{:S(2)}) collective-permute-start(f32[4,128,128]{2,1,0:T(8,128)} %add.39), channel_id=1, source_target_pairs={{0,8},{8,16},{16,24},{24,32},{32,40},{40,48},{48,56},{56,64},{64,7... | collective-permute-start | bytes 786440 | tf_op jit(solution)/shard_map/while/body/eval_jaxpr/ppermute | solution.py:14
  340.9 12.6 %collective-permute-start = (f32[4,128,128]{2,1,0:T(8,128)}, f32[4,128,128]{2,1,0:T(8,128)S(1)}, u32[]{:S(2)}, u32[]{:S(2)}) collective-permute-start(f32[4,128,128]{2,1,0:T(8,128)} %add.39), channel_id=1, source_target_pairs={{0,8},{8,16},{16,24},{24,32},{32,40},{40,48},{48,56},{56,64},{64,7... | collective-permute-start | bytes 786440 | tf_op jit(solution)/shard_map/while/body/eval_jaxpr/ppermute | solution.py:14
  355.2 13.8 %collective-permute-start = (f32[4,128,128]{2,1,0:T(8,128)}, f32[4,128,128]{2,1,0:T(8,128)S(1)}, u32[]{:S(2)}, u32[]{:S(2)}) collective-permute-start(f32[4,128,128]{2,1,0:T(8,128)} %add.39), channel_id=1, source_target_pairs={{0,8},{8,16},{16,24},{24,32},{32,40},{40,48},{48,56},{56,64},{64,7... | collective-permute-start | bytes 786440 | tf_op jit(solution)/shard_map/while/body/eval_jaxpr/ppermute | solution.py:14
  370.6 14.3 %collective-permute-start = (f32[4,128,128]{2,1,0:T(8,128)}, f32[4,128,128]{2,1,0:T(8,128)S(1)}, u32[]{:S(2)}, u32[]{:S(2)}) collective-permute-start(f32[4,128,128]{2,1,0:T(8,128)} %add.39), channel_id=1, source_target_pairs={{0,8},{8,16},{16,24},{24,32},{32,40},{40,48},{48,56},{56,64},{64,7... | collective-permute-start | bytes 786440 | tf_op jit(solution)/shard_map/while/body/eval_jaxpr/ppermute | solution.py:14
  386.5 13.4 %collective-permute-start = (f32[4,128,128]{2,1,0:T(8,128)}, f32[4,128,128]{2,1,0:T(8,128)S(1)}, u32[]{:S(2)}, u32[]{:S(2)}) collective-permute-start(f32[4,128,128]{2,1,0:T(8,128)} %add.39), channel_id=1, source_target_pairs={{0,8},{8,16},{16,24},{24,32},{32,40},{40,48},{48,56},{56,64},{64,7... | collective-permute-start | bytes 786440 | tf_op jit(solution)/shard_map/while/body/eval_jaxpr/ppermute | solution.py:14
  401.6 12.5 %collective-permute-start = (f32[4,128,128]{2,1,0:T(8,128)}, f32[4,128,128]{2,1,0:T(8,128)S(1)}, u32[]{:S(2)}, u32[]{:S(2)}) collective-permute-start(f32[4,128,128]{2,1,0:T(8,128)} %add.39), channel_id=1, source_target_pairs={{0,8},{8,16},{16,24},{24,32},{32,40},{40,48},{48,56},{56,64},{64,7... | collective-permute-start | bytes 786440 | tf_op jit(solution)/shard_map/while/body/eval_jaxpr/ppermute | solution.py:14
  415.8 11.8 %collective-permute-start = (f32[4,128,128]{2,1,0:T(8,128)}, f32[4,128,128]{2,1,0:T(8,128)S(1)}, u32[]{:S(2)}, u32[]{:S(2)}) collective-permute-start(f32[4,128,128]{2,1,0:T(8,128)} %add.39), channel_id=1, source_target_pairs={{0,8},{8,16},{16,24},{24,32},{32,40},{40,48},{48,56},{56,64},{64,7... | collective-permute-start | bytes 786440 | tf_op jit(solution)/shard_map/while/body/eval_jaxpr/ppermute | solution.py:14
  429.2 11.8 %collective-permute-start = (f32[4,128,128]{2,1,0:T(8,128)}, f32[4,128,128]{2,1,0:T(8,128)S(1)}, u32[]{:S(2)}, u32[]{:S(2)}) collective-permute-start(f32[4,128,128]{2,1,0:T(8,128)} %add.39), channel_id=1, source_target_pairs={{0,8},{8,16},{16,24},{24,32},{32,40},{40,48},{48,56},{56,64},{64,7... | collective-permute-start | bytes 786440 | tf_op jit(solution)/shard_map/while/body/eval_jaxpr/ppermute | solution.py:14
  442.7 11.8 %collective-permute-start = (f32[4,128,128]{2,1,0:T(8,128)}, f32[4,128,128]{2,1,0:T(8,128)S(1)}, u32[]{:S(2)}, u32[]{:S(2)}) collective-permute-start(f32[4,128,128]{2,1,0:T(8,128)} %add.39), channel_id=1, source_target_pairs={{0,8},{8,16},{16,24},{24,32},{32,40},{40,48},{48,56},{56,64},{64,7... | collective-permute-start | bytes 786440 | tf_op jit(solution)/shard_map/while/body/eval_jaxpr/ppermute | solution.py:14
  456.1 11.8 %collective-permute-start = (f32[4,128,128]{2,1,0:T(8,128)}, f32[4,128,128]{2,1,0:T(8,128)S(1)}, u32[]{:S(2)}, u32[]{:S(2)}) collective-permute-start(f32[4,128,128]{2,1,0:T(8,128)} %add.39), channel_id=1, source_target_pairs={{0,8},{8,16},{16,24},{24,32},{32,40},{40,48},{48,56},{56,64},{64,7... | collective-permute-start | bytes 786440 | tf_op jit(solution)/shard_map/while/body/eval_jaxpr/ppermute | solution.py:14
  469.6 11.8 %collective-permute-start = (f32[4,128,128]{2,1,0:T(8,128)}, f32[4,128,128]{2,1,0:T(8,128)S(1)}, u32[]{:S(2)}, u32[]{:S(2)}) collective-permute-start(f32[4,128,128]{2,1,0:T(8,128)} %add.39), channel_id=1, source_target_pairs={{0,8},{8,16},{16,24},{24,32},{32,40},{40,48},{48,56},{56,64},{64,7... | collective-permute-start | bytes 786440 | tf_op jit(solution)/shard_map/while/body/eval_jaxpr/ppermute | solution.py:14
  483.0 11.8 %collective-permute-start = (f32[4,128,128]{2,1,0:T(8,128)}, f32[4,128,128]{2,1,0:T(8,128)S(1)}, u32[]{:S(2)}, u32[]{:S(2)}) collective-permute-start(f32[4,128,128]{2,1,0:T(8,128)} %add.39), channel_id=1, source_target_pairs={{0,8},{8,16},{16,24},{24,32},{32,40},{40,48},{48,56},{56,64},{64,7... | collective-permute-start | bytes 786440 | tf_op jit(solution)/shard_map/while/body/eval_jaxpr/ppermute | solution.py:14
  497.5 4.2 copy-start.2
